TPU v7x, 256 devices: a whole 4x4x8 slice. The times are simulated.
256 devices in a mesh: dp: 16 (over z_lo, y), tensor: 16 (over x, z_hi, core).
Axes of the slice: x: 4, y: 4, z: 8 (z_hi: 2, z_lo: 4; z = z_hi * 4 + z_lo), core: 2. Of those that a mesh axis runs over, the one named last changes fastest.
Arguments:
- hidden: bfloat16 [12288, 2048], P(('dp', 'tensor')), may hold values from -6 to 6
- lengths: int32 [64], replicated, may hold values from 1 to 384, as said below
- prefix_id: int32 [64], replicated, may hold values from 0 to 1
- placement_perm: int32 [64], replicated, may hold values from 0 to 63, as said below
- prefix_owner: int32 [2], replicated, may hold values from 0 to 15, as said below
- prefix_cache: bfloat16 [16, 2, 4096, 2048], P('dp', None, None, 'tensor'), may hold values from -400 to 400
- qkv_weight: bfloat16 [3, 2048, 2048], P(None, None, 'tensor')
- q_gain: float32 [2048], replicated, may hold values from 0.1 to 1.9
- k_gain: float32 [2048], replicated, may hold values from 0.1 to 1.9
- out_weight: bfloat16 [2048, 2048], P('tensor'), may hold values from -0.125 to 0.125
- attn_gain: float32 [2048], replicated, may hold values from 0.1 to 1.9
- gate_up_weight: bfloat16 [2, 2048, 8192], P(None, None, 'tensor'), may hold values from -0.125 to 0.125
- down_weight: bfloat16 [8192, 2048], P('tensor'), may hold values from -0.0625 to 0.0625
- mlp_gain: float32 [2048], replicated, may hold values from 0.1 to 1.9
Outputs:
- hidden_out: bfloat16 [12288, 2048], P(('dp', 'tensor'))
- suffix_kv: bfloat16 [2, 12288, 2048], P(None, 'dp', 'tensor')
Inputs may be any that keep to these rules, and one draw needn't show every extreme that they name: `lengths`: the requests that placement_perm puts into one group hold at most 768 tokens together; in every draw some group holds exactly 768. `placement_perm`: A permutation of the 64 requests. `prefix_owner`: two different dp indices, one of which is always the last dp index.
All inputs are finite; a program needn't handle non-finite values.
Results may differ from a plain program's by a relative error of at most 0.025.
Values may be sent and summed in bfloat16 or wider, within the bound.
No kernel may reach another device: no remote copies, remote signals or barrier semaphores. Data moves between devices by JAX's collectives and lax.ppermute only.
A program may use at most 128 MiB of HBM per device.

v0:
```python
import jax
import jax.numpy as jnp
from jax import lax
from jax.sharding import PartitionSpec as P

D = 2048
HD = 128
CAP = 768
REQ_GRP = 4
PLEN = 4096
ROPE_BASE = 500000.0
EPSILON = 1e-06
MASKED_SCORE = -1e30


def from_root(shard, axis, root):
    mine = lax.axis_index(axis) == root
    return lax.psum(jnp.where(mine, shard, jnp.zeros_like(shard)), axis)


def slot_plan(lengths, prefix_id, placement_perm, group_index):
    requests = lax.dynamic_slice(placement_perm, (group_index * REQ_GRP,), (REQ_GRP,))
    req_sizes = jnp.take(lengths, requests)
    starts = jnp.cumsum(req_sizes) - req_sizes
    slot_ids = jnp.arange(CAP, dtype=jnp.int32)
    inside = (
        (slot_ids[None, :] >= starts[:, None]) & (slot_ids[None, :] < (starts + req_sizes)[:, None])
    ).astype(jnp.int32)
    live_slots = jnp.sum(inside, axis=0) > 0
    numbers = jnp.arange(1, REQ_GRP + 1, dtype=jnp.int32)
    owner_req = jnp.sum(inside * numbers[:, None], axis=0) - 1
    offsets = slot_ids - jnp.sum(inside * starts[:, None], axis=0)
    prefix_pick = jnp.sum(inside * jnp.take(prefix_id, requests)[:, None], axis=0)
    return (slot_ids, live_slots, owner_req, offsets, prefix_pick)


def rotate(values, offsets):
    half_dim = HD // 2
    inverse = jnp.power(ROPE_BASE, -2.0 * jnp.arange(half_dim, dtype=jnp.float32) / HD)
    angles = (offsets.astype(jnp.float32) + PLEN)[:, None] * inverse[None, :]
    cosine = jnp.cos(angles)[:, None, :]
    sine_part = jnp.sin(angles)[:, None, :]
    front_half = values[..., :half_dim]
    back_half = values[..., half_dim:]
    return jnp.concatenate(
        [front_half * cosine - back_half * sine_part, back_half * cosine + front_half * sine_part],
        axis=-1,
    )


def rms_scale(values, gain):
    mean_square = jnp.mean(values * values, axis=-1, keepdims=True)
    return values * lax.rsqrt(mean_square + EPSILON) * gain


def partial_softmax(scores, value_heads):
    running_max = jnp.max(scores, axis=-1, keepdims=True)
    weights = jnp.exp(scores - running_max)
    weight_sum = jnp.sum(weights, axis=-1, keepdims=True)
    accumulated = jnp.einsum(
        "hck,khd->hcd",
        weights.astype(jnp.bfloat16),
        value_heads,
        preferred_element_type=jnp.float32,
    )
    return (running_max, weight_sum, accumulated)


def merge_partials(partials):
    running_max = partials[0][0]
    for member in partials[1:]:
        running_max = jnp.maximum(running_max, member[0])
    weight_sum = jnp.zeros_like(partials[0][1])
    accumulated = jnp.zeros_like(partials[0][2])
    for member in partials:
        factor = jnp.exp(member[0] - running_max)
        weight_sum = weight_sum + factor * member[1]
        accumulated = accumulated + factor * member[2]
    return accumulated / weight_sum


def body(
    hidden,
    lengths,
    prefix_id,
    placement_perm,
    prefix_owner,
    prefix_cache,
    qkv_weight,
    q_gain,
    k_gain,
    out_weight,
    attn_gain,
    gate_up_weight,
    down_weight,
    mlp_gain,
):
    tensor_rank = lax.axis_index("tensor")
    group_index = lax.axis_index("dp")
    slot_ids, live_slots, owner_req, offsets, prefix_pick = slot_plan(
        lengths, prefix_id, placement_perm, group_index
    )
    local_rows = hidden.shape[0]
    local_width = qkv_weight.shape[2]
    local_heads = local_width // HD
    row_start = tensor_rank * local_rows
    column_start = tensor_rank * local_width
    score_scale = HD ** (-0.5)
    full_rows = lax.all_gather(hidden, "tensor", axis=0, tiled=True)
    projected = jnp.einsum("cd,kde->kce", full_rows, qkv_weight, preferred_element_type=jnp.float32)
    norm_gains = jnp.stack(
        [
            lax.dynamic_slice_in_dim(q_gain, column_start, local_width),
            lax.dynamic_slice_in_dim(k_gain, column_start, local_width),
        ]
    )
    squares = jnp.sum(projected[:2] * projected[:2], axis=2)
    totals = lax.psum(squares, "tensor")
    normed = projected[:2] * lax.rsqrt(totals / D + EPSILON)[:, :, None] * norm_gains[:, None, :]
    queries = rotate(normed[0].reshape(CAP, local_heads, HD), offsets).astype(jnp.bfloat16)
    key_heads = rotate(normed[1].reshape(CAP, local_heads, HD), offsets).astype(jnp.bfloat16)
    value_heads = projected[2].astype(jnp.bfloat16).reshape(CAP, local_heads, HD)
    suf_scores = (
        jnp.einsum("chd,khd->hck", queries, key_heads, preferred_element_type=jnp.float32)
        * score_scale
    )
    visible = (
        (owner_req[:, None] == owner_req[None, :])
        & live_slots[None, :]
        & (slot_ids[None, :] <= slot_ids[:, None])
    )
    suf_scores = jnp.where(visible[None], suf_scores, MASKED_SCORE)
    partials = [partial_softmax(suf_scores, value_heads)]
    for prefix_num in range(2):
        prefix_kv = from_root(prefix_cache[0], "dp", prefix_owner[prefix_num])
        prefix_keys = prefix_kv[0].reshape(PLEN, local_heads, HD)
        prefix_values = prefix_kv[1].reshape(PLEN, local_heads, HD)
        pre_scores = (
            jnp.einsum("chd,khd->hck", queries, prefix_keys, preferred_element_type=jnp.float32)
            * score_scale
        )
        pre_scores = jnp.where((prefix_pick == prefix_num)[None, :, None], pre_scores, MASKED_SCORE)
        partials.append(partial_softmax(pre_scores, prefix_values))
    attended = merge_partials(partials).astype(jnp.bfloat16)
    attended = attended.transpose(1, 0, 2).reshape(CAP, local_width)
    summed = lax.psum(
        jnp.dot(attended, out_weight, preferred_element_type=jnp.float32).astype(jnp.bfloat16),
        "tensor",
    ).astype(jnp.float32)
    merged = (full_rows.astype(jnp.float32) + rms_scale(summed, attn_gain)).astype(jnp.bfloat16)
    mid_rows = lax.dynamic_slice_in_dim(merged, row_start, local_rows, 0)
    gate_up = jnp.einsum("cd,kdf->kcf", merged, gate_up_weight, preferred_element_type=jnp.float32)
    activated = (jax.nn.silu(gate_up[0]) * gate_up[1]).astype(jnp.bfloat16)
    mlp_term = lax.psum_scatter(
        jnp.dot(activated, down_weight, preferred_element_type=jnp.float32).astype(jnp.bfloat16),
        "tensor",
        scatter_dimension=0,
        tiled=True,
    ).astype(jnp.float32)
    result = mid_rows.astype(jnp.float32) + rms_scale(mlp_term, mlp_gain)
    live_rows = lax.dynamic_slice_in_dim(live_slots, row_start, local_rows, 0)
    hidden_out = jnp.where(live_rows[:, None], result, 0.0).astype(jnp.bfloat16)
    key_out = jnp.where(live_slots[:, None], key_heads.reshape(CAP, local_width), 0.0)
    value_out = jnp.where(live_slots[:, None], value_heads.reshape(CAP, local_width), 0.0)
    suffix_kv = jnp.stack([key_out, value_out])
    return (hidden_out, suffix_kv)


def solution(mesh):
    in_specs = (
        P(("dp", "tensor"), None),
        P(),
        P(),
        P(),
        P(),
        P("dp", None, None, "tensor"),
        P(None, None, "tensor"),
        P(),
        P(),
        P("tensor", None),
        P(),
        P(None, None, "tensor"),
        P("tensor", None),
        P(),
    )
    out_specs = (P(("dp", "tensor"), None), P(None, "dp", "tensor"))
    return jax.shard_map(body, mesh=mesh, in_specs=in_specs, out_specs=out_specs, check_vma=False)
```

profile of v0, /device:TPU:8, one launch (start us, length us, event | category | flops | bytes accessed | tf_op | source)
XLA Modules:
  0.0 571.1 jit_solution(1590346645159021836)
XLA Ops:
  8.1 0.7 all-gather.2.cloned.1.call-update
  8.8 1.3 fusion.90
  11.4 4.0 select_bitcast_fusion.1
  15.5 0.6 copy-done.14
  16.1 0.6 gather_fusion
  17.0 0.6 gather_fusion.1
  17.7 0.8 dynamic-slice_bitcast_fusion
  18.7 65.7 %all-gather.2.cloned.1.call-done = bf16[768,2048]{1,0:T(8,128)(2,1)} async-done(((bf16[48,2048]{1,0:T(8,128)(2,1)}), bf16[768,2048]{1,0:T(8,128)(2,1)}) %all-gather.2.cloned.1.call-update) | async-done | bytes 3145744 | tf_op jit(solution)/shard_map/all_gather | solution.py:109
  84.5 3.8 fusion.26
  88.3 43.7 %psum.28 = f32[2,768]{1,0:T(2,128)S(1)} all-reduce(f32[2,768]{1,0:T(2,128)S(1)} %multiply_reduce_fusion), channel_id=1, replica_groups=mesh['dp'=16,'tensor'=16] {'tensor'}, use_global_device_ids=true, to_apply=%region_4.6 | all-reduce | flops 1536 | bytes 12288 | tf_op jit(solution)/shard_map/psum | solution.py:118
  132.2 0.8 fusion.67
  133.1 0.6 copy-done.8
  133.7 0.7 fusion.91
  134.5 1.4 copy-done.4
  136.3 78.6 %all-reduce.6.cloned.1.call-done = (bf16[2,4096,128]{2,1,0:T(8,128)(2,1)}, bf16[2,4096,128]{2,1,0:T(8,128)(2,1)}) async-done(((bf16[2,4096,128]{2,1,0:T(8,128)(2,1)}, bf16[2,4096,128]{2,1,0:T(8,128)(2,1)}), (bf16[2,4096,128]{2,1,0:T(8,128)(2,1)}, bf16[2,4096,128]{2,1,0:T(8,128)(2,1)})) %all-reduce.6.cloned.1.call-update) | async-done | bytes 4194320 | tf_op jit(solution)/shard_map/psum | solution.py:18
  214.9 4.5 fusion
  219.4 3.2 fusion.2
  222.5 3.2 fusion.1
  225.7 3.4 fusion.4
  229.1 3.5 fusion.32
  232.7 3.5 fusion.35
  236.1 5.6 convolution_convert_fusion.1
  242.1 208.5 %all-reduce.4.cloned.1.call-done = bf16[768,2048]{1,0:T(8,128)(2,1)} async-done(((bf16[768,2048]{1,0:T(8,128)(2,1)}), bf16[768,2048]{1,0:T(8,128)(2,1)}) %all-reduce.4.cloned.1.call-update) | async-done | bytes 3145744 | tf_op jit(solution)/shard_map/psum | solution.py:146
  450.6 2.7 fusion.6
  453.5 3.8 fusion.9
  457.3 3.4 fusion.21
  460.8 3.5 convolution_convert_fusion
  464.4 0.8 copy-done.9
  465.3 0.9 copy.21
  466.3 94.8 %reduce-scatter.2.cloned.1.call-done = bf16[48,2048]{1,0:T(8,128)(2,1)} async-done(((bf16[768,2048]{1,0:T(8,128)(2,1)}), bf16[48,2048]{1,0:T(8,128)(2,1)}) %reduce-scatter.2.cloned.1.call-update) | async-done | bytes 196624 | tf_op jit(solution)/shard_map/reduce_scatter | solution.py:154
  561.0 1.1 fusion.49
  562.1 1.9 fusion.53
  (58 shorter events, 2.1 us)
Async XLA Ops:
  8.0 452.8 %copy-start = (bf16[512,2048]{1,0:T(8,128)(2,1)S(1)}, bf16[512,2048]{1,0:T(8,128)(2,1)}, u32[]{:S(2)}) copy-start(bf16[512,2048]{1,0:T(8,128)(2,1)} %param.28) | copy-start | bytes 6291460
  8.0 76.4 %all-gather.2.cloned.1.call-start = ((), (), s32[]{:S(2)}) async-start(), calls=%async_computation.1 | async-start | bytes 3342336 | tf_op jit(solution)/shard_map/all_gather | solution.py:109
  8.7 206.2 %all-reduce.6.cloned.1.call-start = ((), (), s32[]{:S(2)}) async-start(), calls=%async_computation.4 | async-start | bytes 8388608 | tf_op jit(solution)/shard_map/psum | solution.py:18
  15.4 0.7 copy-start.14
  15.4 0.7 copy-start.1
  15.4 1.6 copy-start.2
  15.4 435.2 %all-reduce.4.cloned.1.call-start = ((), (), s32[]{:S(2)}) async-start(), calls=%async_computation.2 | async-start | bytes 6291456 | tf_op jit(solution)/shard_map/psum | solution.py:146
  133.1 0.6 copy-start.8
  133.1 1.4 copy-start.10
  134.5 1.5 copy-start.4
  219.4 3.2 copy-start.6
  225.7 3.4 copy-start.7
  241.8 211.6 %copy-start.12 = (f32[2048]{0:T(1024)S(1)}, f32[2048]{0:T(1024)}, u32[]{:S(2)}) copy-start(f32[2048]{0:T(1024)} %param.26) | copy-start | bytes 24580
  241.8 319.3 %reduce-scatter.2.cloned.1.call-start = ((), (), s32[]{:S(2)}) async-start(), calls=%async_computation.3 | async-start | bytes 3342336 | tf_op jit(solution)/shard_map/reduce_scatter | solution.py:154
  450.6 2.8 copy-start.3
  453.5 3.9 copy-start.15
  457.3 3.4 copy-start.5
  464.3 0.9 copy-start.9
  464.3 0.9 copy-start.11
  464.3 97.8 %copy-start.13 = (f32[2048]{0:T(1024)S(1)}, f32[2048]{0:T(1024)}, u32[]{:S(2)}) copy-start(f32[2048]{0:T(1024)} %param.29) | copy-start | bytes 24580
Sparse Core Ops, SparseCore 0:
  11.5 72.8 all-gather.1
  241.9 208.6 all-reduce.3
  464.4 96.5 reduce-scatter.1
Sparse Core Ops, SparseCore 1:
  15.5 199.3 all-reduce.5
where the time goes:
time: 571 us
  waiting for transfers between devices  448 us (78%)
  blocking collectives  43.7 us (8%)
  matrix products  31.7 us (6%)
  other arithmetic  22.2 us (4%)
  between operations  16.8 us (3%)
  local copies, waits for them, and re-layouts  8.02 us (1%)
    psum x1, waiting for transfers between devices, body(): lax.psum(jnp.dot(attended, out_weight, preferred_element_type=jnp.float32...  209 us
    reduce_scatter x1, waiting for transfers between devices, body(): lax.psum_scatter(jnp.dot(activated, down_weight, preferred_element_type=j...  94.8 us
    psum x1, waiting for transfers between devices, from_root(): return lax.psum(jnp.where(mine, shard, jnp.zeros_like(shard)), axis)  78.6 us
    all_gather x1, waiting for transfers between devices, body(): full_rows = lax.all_gather(hidden, 'tensor', axis=0, tiled=True)  65.7 us
    psum x1, blocking collectives, body(): totals = lax.psum(squares, 'tensor')  43.7 us
  transfers between devices with their start and end apart: 4, of which 4 were waited for; matrix products, arithmetic and copies ran while one was open for 3% of the time, Pallas kernels for 0%

commit v1 on v0

--- a/solution.py
+++ b/solution.py
@@ -2,6 +2,7 @@
 import jax.numpy as jnp
 from jax import lax
 from jax.sharding import PartitionSpec as P
+from jax.lax import all_to_all, axis_size
 
 D = 2048
 HD = 128
@@ -106,7 +107,12 @@
     row_start = tensor_rank * local_rows
     column_start = tensor_rank * local_width
     score_scale = HD ** (-0.5)
-    full_rows = lax.all_gather(hidden, "tensor", axis=0, tiled=True)
+    full_rows = jnp.concatenate(
+        all_to_all(
+            jnp.stack([hidden] * axis_size("tensor"), axis=0), "tensor", split_axis=0, concat_axis=0
+        ),
+        0,
+    )
     projected = jnp.einsum("cd,kde->kce", full_rows, qkv_weight, preferred_element_type=jnp.float32)
     norm_gains = jnp.stack(
         [

time: 571 us -> 600 us (1.051)
  waiting for transfers between devices: 448 us -> 464 us
  starting transfers between devices: 0.42 us -> 11.6 us
    all_to_all x0 -> x1, waiting for transfers between devices: none -> 66.8 us  [body(): all_to_all(jnp.stack([hidden] * axis_size('tensor'), axis=0), 'tensor', s...]
    all_gather x1 -> x0, waiting for transfers between devices: 65.7 us -> none  [body(): full_rows = lax.all_gather(hidden, 'tensor', axis=0, tiled=True)]
    all_to_all x0 -> x1, starting transfers between devices: none -> 11.2 us  [body(): all_to_all(jnp.stack([hidden] * axis_size('tensor'), axis=0), 'tensor', s...]
    psum x1, waiting for transfers between devices: 78.6 us -> 89.8 us  [from_root(): return lax.psum(jnp.where(mine, shard, jnp.zeros_like(shard)), axis)]
  transfers between devices with their start and end apart: 4 -> 4, of which waited for: 4 -> 4; matrix products, arithmetic and copies ran while one was open for 3% -> 2% of each run, Pallas kernels for 0% -> 0%
where the time goes in v1:
time: 600 us
  waiting for transfers between devices  464 us (77%)
  blocking collectives  43.6 us (7%)
  matrix products  33 us (6%)
  other arithmetic  22.8 us (4%)
  between operations  15.3 us (3%)
  starting transfers between devices  11.6 us (2%)
  local copies, waits for them, and re-layouts  9.8 us (2%)
    psum x1, waiting for transfers between devices, body(): lax.psum(jnp.dot(attended, out_weight, preferred_element_type=jnp.float32...  212 us
    reduce_scatter x1, waiting for transfers between devices, body(): lax.psum_scatter(jnp.dot(activated, down_weight, preferred_element_type=j...  94.8 us
    psum x1, waiting for transfers between devices, from_root(): return lax.psum(jnp.where(mine, shard, jnp.zeros_like(shard)), axis)  89.8 us
    all_to_all x1, waiting for transfers between devices, body(): all_to_all(jnp.stack([hidden] * axis_size('tensor'), axis=0), 'tensor', s...  66.8 us
    psum x1, blocking collectives, body(): totals = lax.psum(squares, 'tensor')  43.6 us
  transfers between devices with their start and end apart: 4, of which 4 were waited for; matrix products, arithmetic and copies ran while one was open for 2% of the time, Pallas kernels for 0%

profile of v1, /device:TPU:8, one launch (start us, length us, event | category | flops | bytes accessed | tf_op | source)
XLA Modules:
  0.0 600.0 jit_solution(10426058517906021504)
XLA Ops:
  7.2 3.1 stack.10
  10.3 11.2 %all-to-all-start = ((bf16[16,48,2048]{2,1,0:T(8,128)(2,1)}), bf16[16,48,2048]{2,1,0:T(8,128)(2,1)}, u32[]{:S(2)}, u32[]{:S(2)}) async-start(bf16[16,48,2048]{2,1,0:T(8,128)(2,1)} %stack.10), calls=%async_computation | async-start | bytes 6291456 | tf_op jit(solution)/shard_map/all_to_all | solution.py:111
  21.6 0.6 fusion.85
  23.5 3.9 select_bitcast_fusion.1
  27.5 0.6 copy-done.14
  28.1 0.6 gather_fusion
  29.1 0.6 gather_fusion.1
  29.7 0.8 dynamic-slice_bitcast_fusion
  30.7 66.8 %all-to-all-done = bf16[16,48,2048]{2,1,0:T(8,128)(2,1)} async-done(((bf16[16,48,2048]{2,1,0:T(8,128)(2,1)}), bf16[16,48,2048]{2,1,0:T(8,128)(2,1)}, u32[]{:S(2)}, u32[]{:S(2)}) %all-to-all-start) | async-done | bytes 3145760 | tf_op jit(solution)/shard_map/all_to_all | solution.py:111
  97.6 3.8 convolution_bitcast_fusion
  101.5 43.6 %psum.28 = f32[2,768]{1,0:T(2,128)S(1)} all-reduce(f32[2,768]{1,0:T(2,128)S(1)} %multiply_reduce_fusion), channel_id=1, replica_groups=mesh['dp'=16,'tensor'=16] {'tensor'}, use_global_device_ids=true, to_apply=%region_4.6 | all-reduce | flops 1536 | bytes 12288 | tf_op jit(solution)/shard_map/psum | solution.py:124
  145.4 1.5 fusion.62
  146.9 89.8 %all-reduce.6.cloned.1.call-done = (bf16[2,4096,128]{2,1,0:T(8,128)(2,1)}, bf16[2,4096,128]{2,1,0:T(8,128)(2,1)}) async-done(((bf16[2,4096,128]{2,1,0:T(8,128)(2,1)}, bf16[2,4096,128]{2,1,0:T(8,128)(2,1)}), (bf16[2,4096,128]{2,1,0:T(8,128)(2,1)}, bf16[2,4096,128]{2,1,0:T(8,128)(2,1)})) %all-reduce.6.cloned.1.call-update) | async-done | bytes 4194320 | tf_op jit(solution)/shard_map/psum | solution.py:19
  236.7 4.5 fusion.1
  241.1 3.2 fusion.4
  244.3 3.1 fusion
  247.5 3.4 fusion.2
  250.9 0.7 fusion.86
  251.7 1.4 copy-done.4
  253.5 4.8 fusion.30
  258.2 3.5 fusion.27
  261.8 5.6 convolution_convert_fusion.1
  267.7 212.5 %all-reduce.4.cloned.1.call-done = bf16[768,2048]{1,0:T(8,128)(2,1)} async-done(((bf16[768,2048]{1,0:T(8,128)(2,1)}), bf16[768,2048]{1,0:T(8,128)(2,1)}) %all-reduce.4.cloned.1.call-update) | async-done | bytes 3145744 | tf_op jit(solution)/shard_map/psum | solution.py:152
  480.2 2.7 fusion.6
  483.0 3.8 fusion.9
  486.9 3.4 fusion.19
  490.3 3.5 convolution_convert_fusion
  493.9 0.8 copy-done.8
  494.9 0.9 copy.21
  495.8 94.8 %reduce-scatter.2.cloned.1.call-done = bf16[48,2048]{1,0:T(8,128)(2,1)} async-done(((bf16[768,2048]{1,0:T(8,128)(2,1)}), bf16[48,2048]{1,0:T(8,128)(2,1)}) %reduce-scatter.2.cloned.1.call-update) | async-done | bytes 196624 | tf_op jit(solution)/shard_map/reduce_scatter | solution.py:160
  590.6 1.1 fusion.44
  591.6 1.9 fusion.48
  (58 shorter events, 2.1 us)
Async XLA Ops:
  7.2 483.1 %copy-start = (bf16[512,2048]{1,0:T(8,128)(2,1)S(1)}, bf16[512,2048]{1,0:T(8,128)(2,1)}, u32[]{:S(2)}) copy-start(bf16[512,2048]{1,0:T(8,128)(2,1)} %param.28) | copy-start | bytes 6291460
  10.3 11.3 %copy-start.13 = (s32[2]{0:T(128)S(1)}, s32[2]{0:T(128)}, u32[]{:S(2)}) copy-start(s32[2]{0:T(128)} %param.20) | copy-start | bytes 28
  10.3 87.3 %all-to-all-start = ((bf16[16,48,2048]{2,1,0:T(8,128)(2,1)}), bf16[16,48,2048]{2,1,0:T(8,128)(2,1)}, u32[]{:S(2)}, u32[]{:S(2)}) async-start(bf16[16,48,2048]{2,1,0:T(8,128)(2,1)} %stack.10), calls=%async_computation | async-start | bytes 6291456 | tf_op jit(solution)/shard_map/all_to_all | solution.py:111
  21.5 215.1 %all-reduce.6.cloned.1.call-start = ((), (), s32[]{:S(2)}) async-start(), calls=%async_computation.4 | async-start | bytes 8388608 | tf_op jit(solution)/shard_map/psum | solution.py:19
  27.4 0.7 copy-start.14
  27.4 0.7 copy-start.1
  27.4 1.6 copy-start.2
  27.4 452.7 %all-reduce.4.cloned.1.call-start = ((), (), s32[]{:S(2)}) async-start(), calls=%async_computation.2 | async-start | bytes 6291456 | tf_op jit(solution)/shard_map/psum | solution.py:152
  241.1 3.2 copy-start.6
  247.5 3.4 copy-start.7
  247.5 3.4 copy-start.9
  251.6 1.4 copy-start.4
  267.4 215.5 %copy-start.11 = (f32[2048]{0:T(1024)S(1)}, f32[2048]{0:T(1024)}, u32[]{:S(2)}) copy-start(f32[2048]{0:T(1024)} %param.26) | copy-start | bytes 24580
  267.4 323.2 %reduce-scatter.2.cloned.1.call-start = ((), (), s32[]{:S(2)}) async-start(), calls=%async_computation.3 | async-start | bytes 3342336 | tf_op jit(solution)/shard_map/reduce_scatter | solution.py:160
  480.2 2.8 copy-start.3
  483.0 3.9 copy-start.15
  486.8 3.4 copy-start.5
  493.8 0.9 copy-start.8
  493.8 0.9 copy-start.10
  493.8 97.8 %copy-start.12 = (f32[2048]{0:T(1024)S(1)}, f32[2048]{0:T(1024)}, u32[]{:S(2)}) copy-start(f32[2048]{0:T(1024)} %param.29) | copy-start | bytes 24580
Sparse Core Ops, SparseCore 0:
  27.6 209.0 all-reduce.5
  267.5 212.6 all-reduce.3
  494.0 96.5 reduce-scatter.1
